TPU v7x, 256 devices: a whole 4x4x8 slice. The times are simulated.
256 devices in a mesh: row: 16 (over z_hi, x, core), col: 16 (over y, z_lo).
Axes of the slice: x: 4, y: 4, z: 8 (z_hi: 2, z_lo: 4; z = z_hi * 4 + z_lo), core: 2. Of those that a mesh axis runs over, the one named last changes fastest.
Arguments:
- points: float32 [64, 32768], P(None, ('row', 'col')), may hold values from -24 to 24, as said below
- embedding: float32 [2, 32768], P(None, ('row', 'col')), may hold values from -8 to 8
- precision: float32 [32768], P(('row', 'col')), may hold values from 0.05 to 2
Outputs:
- force: float32 [2, 32768], P(None, ('row', 'col'))
- calibrated: float32 [32768], P(('row', 'col'))
Inputs may be any that keep to these rules, and one draw needn't show every extreme that they name: `points`: each point's coordinates are normal values times a positive scale of that point.
All inputs are finite; a program needn't handle non-finite values.
Results may differ from a plain program's by a relative error of at most 0.0003.
Values sent between devices are 32-bit elements; how exact they have to be, the bound alone decides.
No kernel may reach another device: no remote copies, remote signals or barrier semaphores. Data moves between devices by JAX's collectives and lax.ppermute only.
A program may use at most 64 MiB of HBM per device.

v0:
```python
import math
import jax
import jax.numpy as jnp
from jax import lax
from jax.sharding import PartitionSpec as P

PERP = 30


def newton_update(zsum, first, second, start_prec):
    entropy = jnp.log(zsum) + start_prec * first / zsum
    spread = second / zsum - (first / zsum) ** 2
    factor = jnp.clip(
        (entropy - math.log(PERP)) / jnp.maximum(start_prec * start_prec * spread, 1.0), -2.0, 2.0
    )
    return start_prec * jnp.exp(factor)


def body(points, embedding, precision):
    per_dev = points.shape[1]
    width = points.shape[0]
    col_count = lax.axis_size("col")
    row_count = lax.axis_size("row")
    packed = jnp.concatenate([points, embedding, precision[None, :]], axis=0)
    row_pack = lax.all_gather(packed, "col", axis=1, tiled=True)
    col_pack = lax.all_gather(packed, "row", axis=1, tiled=True)
    rows_total = per_dev * col_count
    cols_total = per_dev * row_count
    total = rows_total * row_count
    row_coords = row_pack[:width]
    col_coords = col_pack[:width]
    row_map = row_pack[width : width + 2]
    col_map = col_pack[width : width + 2]
    row_prec = row_pack[width + 2]
    row_sq = jnp.sum(row_coords * row_coords, axis=0)
    col_sq = jnp.sum(col_coords * col_coords, axis=0)
    row_ids = lax.axis_index("row") * rows_total + jnp.arange(rows_total, dtype=jnp.int32)
    col_pos = jnp.arange(cols_total, dtype=jnp.int32)
    col_ids = col_pos // per_dev * rows_total + lax.axis_index("col") * per_dev + col_pos % per_dev
    block_rows = min(rows_total, 256)
    blocks = rows_total // block_rows
    own_start = lax.axis_index("col") * per_dev

    def slice_rows(values, start):
        return lax.dynamic_slice_in_dim(values, start, block_rows, values.ndim - 1)

    def distances(start):
        part = slice_rows(row_coords, start)
        inner = lax.dot_general(
            part,
            col_coords,
            (((0,), (0,)), ((), ())),
            precision=lax.Precision.HIGHEST,
            preferred_element_type=jnp.float32,
        )
        distance = jnp.maximum(
            slice_rows(row_sq, start)[:, None] + col_sq[None, :] - 2.0 * inner, 0.0
        )
        itself = slice_rows(row_ids, start)[:, None] == col_ids[None, :]
        return (distance, itself)

    def kernel_of(start, itself):
        part_y = slice_rows(row_map, start)
        delta_a = part_y[0][:, None] - col_map[0][None, :]
        delta_b = part_y[1][:, None] - col_map[1][None, :]
        return (jnp.where(itself, 0.0, 1.0 / (1.0 + delta_a * delta_a + delta_b * delta_b)), part_y)

    def sweep(step_fn, init):

        def wrapped(carry, index):
            return step_fn(carry, index * block_rows)

        carry, result = lax.scan(wrapped, init, jnp.arange(blocks, dtype=jnp.int32))
        return (carry, result.transpose(1, 0, 2).reshape(result.shape[1], rows_total))

    def nearest_step(carry, start):
        distance, itself = distances(start)
        masked = jnp.where(itself, jnp.inf, distance)
        return (carry, jnp.min(masked, axis=1)[None])

    col_min_part, row_min_part = sweep(nearest_step, jnp.full((cols_total,), jnp.inf, jnp.float32))
    nearest_rows = lax.pmin(row_min_part[0], "col")

    def moment_step(carry, start):
        distance, itself = distances(start)
        shifted = distance - slice_rows(nearest_rows, start)[:, None]
        expo = jnp.where(itself, 0.0, jnp.exp(-slice_rows(row_prec, start)[:, None] * shifted))
        row_part = jnp.stack(
            [
                jnp.sum(expo, axis=1),
                jnp.sum(expo * shifted, axis=1),
                jnp.sum(expo * shifted * shifted, axis=1),
            ]
        )
        return (carry, row_part)

    col_moment, row_moment = sweep(moment_step, jnp.zeros((3, cols_total), jnp.float32))
    row_z, row_first, row_second = lax.psum((row_moment[0], row_moment[1], row_moment[2]), "col")
    calib_rows = newton_update(row_z, row_first, row_second, row_prec)

    def norm_step(carry, start):
        distance, itself = distances(start)
        shifted = distance - slice_rows(nearest_rows, start)[:, None]
        row_part = jnp.sum(
            jnp.where(itself, 0.0, jnp.exp(-slice_rows(calib_rows, start)[:, None] * shifted)),
            axis=1,
        )
        return (carry, row_part[None])

    col_norm_part, row_norm_part = sweep(norm_step, jnp.zeros((cols_total,), jnp.float32))
    norm_rows = lax.psum(row_norm_part[0], "col")
    own_stats = jnp.stack(
        [
            lax.dynamic_slice_in_dim(calib_rows, own_start, per_dev, 0),
            lax.dynamic_slice_in_dim(nearest_rows, own_start, per_dev, 0),
            lax.dynamic_slice_in_dim(norm_rows, own_start, per_dev, 0),
        ]
    )
    col_stats = lax.all_gather(own_stats, "row", axis=1, tiled=True)
    calib_cols = col_stats[0]
    nearest_cols = col_stats[1]
    norm_cols = col_stats[2]

    def kernel_step(carry, index):
        start = index * block_rows
        itself = slice_rows(row_ids, start)[:, None] == col_ids[None, :]
        kernel, part_y = kernel_of(start, itself)
        return (carry + jnp.sum(kernel), None)

    kernel_part, unused = lax.scan(
        kernel_step, jnp.zeros((), jnp.float32), jnp.arange(blocks, dtype=jnp.int32)
    )
    qsum = lax.psum(kernel_part, ("row", "col"))

    def pulled(coef, part_y):
        moved = lax.dot_general(
            col_map,
            coef,
            (((1,), (1,)), ((), ())),
            precision=lax.Precision.HIGHEST,
            preferred_element_type=jnp.float32,
        )
        return part_y * jnp.sum(coef, axis=1)[None, :] - moved

    def force_step(carry, start):
        distance, itself = distances(start)
        kernel, part_y = kernel_of(start, itself)
        cond_rows = (
            jnp.exp(
                -slice_rows(calib_rows, start)[:, None]
                * (distance - slice_rows(nearest_rows, start)[:, None])
            )
            / slice_rows(norm_rows, start)[:, None]
        )
        cond_cols = (
            jnp.exp(-calib_cols[None, :] * (distance - nearest_cols[None, :])) / norm_cols[None, :]
        )
        affinity = jnp.where(itself, 0.0, 0.5 * (cond_rows + cond_cols))
        coef = (affinity - total * kernel / qsum) * kernel
        return (carry, pulled(coef, part_y))

    kernel_late, force_rows = sweep(force_step, jnp.zeros((), jnp.float32))
    force = lax.psum_scatter(force_rows, "col", scatter_dimension=1, tiled=True)
    calibrated = lax.dynamic_slice_in_dim(calib_rows, own_start, per_dev, 0)
    return (force, calibrated)


def solution(mesh):
    in_specs = (P(None, ("row", "col")), P(None, ("row", "col")), P(("row", "col")))
    out_specs = (P(None, ("row", "col")), P(("row", "col")))
    return jax.shard_map(body, mesh=mesh, in_specs=in_specs, out_specs=out_specs, check_vma=False)
```

profile of v0, /device:TPU:4, one launch (start us, length us, event | category | flops | bytes accessed | tf_op | source)
XLA Modules:
  0.0 634.6 jit_solution(9365061002655801085)
XLA Ops:
  7.2 0.8 pad_maximum_fusion
  8.0 49.5 %all_gather.9 = f32[67,2048]{1,0:T(8,128)S(1)} all-gather(f32[67,128]{1,0:T(8,128)S(1)} %pad_maximum_fusion), channel_id=1, replica_groups=mesh['row'=16,'col'=16] {'col'}, dimensions={1}, use_global_device_ids=true | all-gather | bytes 583168 | tf_op jit(solution)/shard_map/all_gather | solution.py:25
  57.5 25.0 %all_gather.10 = f32[67,2048]{1,0:T(8,128)S(1)} all-gather(f32[67,128]{1,0:T(8,128)S(1)} %pad_maximum_fusion), channel_id=1, replica_groups=mesh['row'=16,'col'=16] {'row'}, dimensions={1}, use_global_device_ids=true | all-gather | bytes 583168 | tf_op jit(solution)/shard_map/all_gather | solution.py:26
  83.3 31.0 %while.57 = (s32[]{:T(128)}, f32[8,1,256]{2,1,0:T(1,128)S(1)}, s32[8]{0:T(128)S(1)}, s32[2048]{0:T(1024)S(1)}, f32[2048]{0:T(1024)S(1)}, /*index=5*/f32[2048]{0:...) while((s32[]{:T(128)}, f32[8,1,256]{2,1,0:T(1,128)S(1)}, ...), condition=%wide.region_4.5_spmd.clone, body=%wide.region_2.4_spmd.clone.sunk | while | flops 406353664 | bytes 623819 | solution.py:73
  84.8 2.3 fusion.130
  88.7 2.3 fusion.130
  92.6 2.3 fusion.130
  96.4 2.3 fusion.130
  100.3 2.3 fusion.130
  104.2 2.3 fusion.130
  108.0 2.3 fusion.130
  111.9 2.3 fusion.130
  114.3 38.7 %pmin.7 = f32[2048]{0:T(1024)S(1)} all-reduce(f32[2048]{0:T(1024)S(1)} %bitcast.134), channel_id=1, replica_groups=mesh['row'=16,'col'=16] {'col'}, use_global_device_ids=true, to_apply=%region_5.6 | all-reduce | flops 2048 | bytes 16384 | tf_op jit(solution)/shard_map/pmin | solution.py:82
  153.0 34.9 %while.58 = (s32[]{:T(128)}, f32[8,3,256]{2,1,0:T(4,128)S(1)}, s32[8]{0:T(128)S(1)}, s32[2048]{0:T(1024)S(1)}, f32[2048]{0:T(1024)S(1)}, /*index=5*/f32[2048]{0:...) while((s32[]{:T(128)}, f32[8,3,256]{2,1,0:T(4,128)S(1)}, ...), condition=%wide.region_10.11_spmd.clone, body=%wide.region_6.10_spmd.clone.sunk | while | flops 409500672 | bytes 637155 | solution.py:73
  154.4 2.9 fusion.133
  158.8 2.9 fusion.133
  163.2 2.9 fusion.133
  167.5 2.9 fusion.133
  171.9 2.9 fusion.133
  176.2 2.9 fusion.133
  180.6 2.9 fusion.133
  185.0 2.9 fusion.133
  188.0 76.5 %all-reduce = (f32[2048]{0:T(1024)S(1)}, f32[2048]{0:T(1024)S(1)}, f32[2048]{0:T(1024)S(1)}) all-reduce(f32[2048]{0:T(1024)S(1)} %bitcast.132, f32[2048]{0:T(1024)S(1)} %bitcast.133, f32[2048]{0:T(1024)S(1)} %bitcast.131), channel_id=1, replica_groups=mesh['row'=16,'col'=16] {'col'}, use_global_device_ids=true, to_apply=%region_12.13 | all-reduce | flops 6144 | bytes 49152 | tf_op jit(solution)/shard_map/psum | solution.py:98
  264.6 33.4 %while.59 = (s32[]{:T(128)}, f32[8,1,256]{2,1,0:T(1,128)S(1)}, s32[8]{0:T(128)S(1)}, s32[2048]{0:T(1024)S(1)}, f32[2048]{0:T(1024)S(1)}, /*index=5*/f32[2048]{0:...) while((s32[]{:T(128)}, f32[8,1,256]{2,1,0:T(1,128)S(1)}, ...), condition=%wide.region_16.17_spmd.clone, body=%wide.region_14.16_spmd.clone.sunk | while | flops 407402496 | bytes 629987 | solution.py:73
  266.2 2.6 fusion.138
  270.3 2.6 fusion.138
  274.5 2.6 fusion.138
  278.7 2.6 fusion.138
  282.9 2.6 fusion.138
  287.1 2.6 fusion.138
  291.2 2.6 fusion.138
  295.4 2.6 fusion.138
  298.0 38.7 %psum.38 = f32[2048]{0:T(1024)S(1)} all-reduce(f32[2048]{0:T(1024)S(1)} %bitcast.135), channel_id=1, replica_groups=mesh['row'=16,'col'=16] {'col'}, use_global_device_ids=true, to_apply=%region_17.18 | all-reduce | flops 2048 | bytes 16384 | tf_op jit(solution)/shard_map/psum | solution.py:111
  336.9 24.7 %all_gather.11 = f32[3,2048]{1,0:T(4,128)S(1)} all-gather(f32[3,128]{1,0:T(4,128)S(1)} %pad_maximum_fusion.1), channel_id=1, replica_groups=mesh['row'=16,'col'=16] {'row'}, dimensions={1}, use_global_device_ids=true | all-gather | bytes 26112 | tf_op jit(solution)/shard_map/all_gather | solution.py:119
  361.7 34.7 %while.60 = (s32[]{:T(128)}, f32[]{:T(128)}, s32[8]{0:T(128)S(1)}, s32[2048]{0:T(1024)S(1)}, f32[2,2048]{1,0:T(2,128)S(1)}, /*index=5*/f32[2,2048]{1,0:T(2,128)S...) while((s32[]{:T(128)}, f32[]{:T(128)}, s32[8]{0:T(128)S(1)}, ...), condition=%wide.region_20.21_spmd.clone, body=%wide.region_18.20_spmd.clone.sunk | while | flops 5273607 | bytes 74971 | solution.py:130
  363.2 2.1 select_reduce_fusion.2
  367.6 2.1 select_reduce_fusion.2
  371.9 2.1 select_reduce_fusion.2
  376.2 2.1 select_reduce_fusion.2
  380.6 2.1 select_reduce_fusion.2
  384.9 2.1 select_reduce_fusion.2
  389.3 2.1 select_reduce_fusion.2
  393.6 2.1 select_reduce_fusion.2
  396.4 79.2 %psum.39 = f32[]{:T(128)} all-reduce(f32[]{:T(128)} %get-tuple-element.407), channel_id=1, replica_groups=mesh['row'=16,'col'=16] {'row','col'}, use_global_device_ids=true, to_apply=%region_21.22 | all-reduce | flops 1 | bytes 8 | tf_op jit(solution)/shard_map/psum | solution.py:133
  475.6 65.4 %while.61 = (s32[]{:T(128)}, f32[8,2,256]{2,1,0:T(2,128)S(1)}, s32[8]{0:T(128)S(1)}, f32[2,2048]{1,0:T(2,128)S(1)}, s32[2048]{0:T(1024)S(1)}, /*index=5*/f32[204...) while((s32[]{:T(128)}, f32[8,2,256]{2,1,0:T(2,128)S(1)}, ...), condition=%wide.region_24.25_spmd.clone, body=%wide.region_22.24_spmd.clone.sunk | while | flops 429423616 | bytes 4926787 | solution.py:73
  477.4 4.6 fusion.146
  482.0 1.7 fusion.147
  485.6 4.6 fusion.146
  490.2 1.7 fusion.147
  493.8 4.6 fusion.146
  498.4 1.7 fusion.147
  502.0 4.6 fusion.146
  506.6 1.7 fusion.147
  510.2 4.6 fusion.146
  514.7 1.7 fusion.147
  518.4 4.6 fusion.146
  522.9 1.7 fusion.147
  526.5 4.6 fusion.146
  531.1 1.7 fusion.147
  534.7 4.6 fusion.146
  539.3 1.7 fusion.147
  541.0 1.4 copy.8
  543.0 83.2 %reduce-scatter.4.cloned.1.call-done = f32[128,2]{1,0:T(8,128)} async-done(((f32[2048,2]{1,0:T(8,128)}), f32[128,2]{1,0:T(8,128)}) %reduce-scatter.4.cloned.1.call-update) | async-done | bytes 1040
  626.3 1.5 copy.9
  (295 shorter events, 39.0 us)
Async XLA Ops:
  7.2 619.1 %reduce-scatter.4.cloned.1.call-start = ((), (), s32[]{:S(2)}) async-start(), calls=%async_computation.1 | async-start | bytes 1114112
  57.5 25.2 %copy-start.1 = (f32[67,2048]{1,0:T(8,128)}, f32[67,2048]{1,0:T(8,128)S(1)}, u32[]{:S(2)}) copy-start(f32[67,2048]{1,0:T(8,128)S(1)} %all_gather.9) | copy-start | bytes 1646596
  82.5 0.8 copy-start
  264.6 97.1 %slice-start = ((f32[67,2048]{1,0:T(8,128)}), f32[2,2048]{1,0:T(2,128)S(1)}, s32[]{:S(2)}) async-start(f32[67,2048]{1,0:T(8,128)} %copy-done), calls=%async_computation.2 | async-start | bytes 32768 | tf_op jit(solution)/shard_map/slice | solution.py:33
  264.6 97.1 %slice-start.1 = ((f32[67,2048]{1,0:T(8,128)}), f32[2,2048]{1,0:T(2,128)S(1)}, s32[]{:S(2)}) async-start(f32[67,2048]{1,0:T(8,128)} %copy-done.1), calls=%async_computation.3 | async-start | bytes 32768 | tf_op jit(solution)/shard_map/slice | solution.py:32
Sparse Core Ops, SparseCore 0:
  542.6 83.6 reduce-scatter.3
where the time goes:
time: 635 us
  blocking collectives  332 us (52%)
  matrix products  113 us (18%)
  waiting for transfers between devices  83.3 us (13%)
  local copies, waits for them, and re-layouts  39.3 us (6%)
  loops' own time  32.9 us (5%)
  other arithmetic  19.9 us (3%)
  between operations  14.2 us (2%)
    dot_general x32, matrix products, distances(): lax.dot_general(part, col_coords, (((0,), (0,)), ((), ())), precision=lax...  98.7 us
    unnamed x2, waiting for transfers between devices  83.3 us
    psum x1, blocking collectives, body(): qsum = lax.psum(kernel_part, ('row', 'col'))  79.2 us
    psum x1, blocking collectives, body(): lax.psum((row_moment[0], row_moment[1], row_moment[2]), 'col')  76.5 us
    all_gather x1, blocking collectives, body(): row_pack = lax.all_gather(packed, 'col', axis=1, tiled=True)  49.5 us
    psum x1, blocking collectives, body(): norm_rows = lax.psum(row_norm_part[0], 'col')  38.7 us
    pmin x1, blocking collectives, body(): nearest_rows = lax.pmin(row_min_part[0], 'col')  38.7 us
    dynamic_slice x40, local copies, waits for them, and re-layouts, sweep(): carry, result = lax.scan(wrapped, init, jnp.arange(blocks, dtype=jnp.int32))  25.5 us
  transfers between devices with their start and end apart: 1, of which 1 were waited for; matrix products, arithmetic and copies ran while one was open for 0% of the time, Pallas kernels for 0%

commit v1 on v0

--- a/solution.py
+++ b/solution.py
@@ -5,6 +5,13 @@
 from jax.sharding import PartitionSpec as P
 
 PERP = 30
+
+
+def start_quotas(inp, comm_axis):
+    reply = jnp.stack([inp for _ in range(lax.axis_size(comm_axis))])
+    low = lax.all_to_all(reply, comm_axis, 0, 0)
+    small = jnp.concatenate(low, 1)
+    return small
 
 
 def newton_update(zsum, first, second, start_prec):
@@ -22,7 +29,7 @@
     col_count = lax.axis_size("col")
     row_count = lax.axis_size("row")
     packed = jnp.concatenate([points, embedding, precision[None, :]], axis=0)
-    row_pack = lax.all_gather(packed, "col", axis=1, tiled=True)
+    row_pack = start_quotas(packed, "col")
     col_pack = lax.all_gather(packed, "row", axis=1, tiled=True)
     rows_total = per_dev * col_count
     cols_total = per_dev * row_count

time: 635 us -> 602 us (0.948)
  blocking collectives: 332 us -> 291 us
  starting transfers between devices: 0.04 us -> 8.68 us
    all_gather x1 -> x0, blocking collectives: 49.5 us -> none  [body(): row_pack = lax.all_gather(packed, 'col', axis=1, tiled=True)]
    all_to_all x0 -> x1, starting transfers between devices: none -> 8.64 us  [start_quotas(): low = lax.all_to_all(reply, comm_axis, 0, 0)]
    pmin x1, blocking collectives: 38.7 us -> 45.2 us  [body(): nearest_rows = lax.pmin(row_min_part[0], 'col')]
  transfers between devices with their start and end apart: 1 -> 2, of which waited for: 1 -> 1; matrix products, arithmetic and copies ran while one was open for 0% -> 0% of each run, Pallas kernels for 0% -> 0%
where the time goes in v1:
time: 602 us; the launch traced here: 601 us
  blocking collectives  291 us (48%)
  matrix products  113 us (19%)
  waiting for transfers between devices  84.3 us (14%)
  local copies, waits for them, and re-layouts  39.2 us (7%)
  loops' own time  31.2 us (5%)
  other arithmetic  19.9 us (3%)
  between operations  14.2 us (2%)
  starting transfers between devices  8.68 us (1%)
    dot_general x32, matrix products, distances(): lax.dot_general(part, col_coords, (((0,), (0,)), ((), ())), precision=lax...  99 us
    unnamed x2, waiting for transfers between devices  84.3 us
    psum x1, blocking collectives, body(): qsum = lax.psum(kernel_part, ('row', 'col'))  77.2 us
    psum x1, blocking collectives, body(): lax.psum((row_moment[0], row_moment[1], row_moment[2]), 'col')  74.6 us
    pmin x1, blocking collectives, body(): nearest_rows = lax.pmin(row_min_part[0], 'col')  45.2 us
    psum x1, blocking collectives, body(): norm_rows = lax.psum(row_norm_part[0], 'col')  38.8 us
    all_gather x1, blocking collectives, body(): col_stats = lax.all_gather(own_stats, 'row', axis=1, tiled=True)  28 us
    all_gather x1, blocking collectives, body(): col_pack = lax.all_gather(packed, 'row', axis=1, tiled=True)  26.6 us
  transfers between devices with their start and end apart: 2, of which 1 were waited for; matrix products, arithmetic and copies ran while one was open for 0% of the time, Pallas kernels for 0%

profile of v1, /device:TPU:4, one launch (start us, length us, event | category | flops | bytes accessed | tf_op | source)
XLA Modules:
  0.0 601.0 jit_solution(14249427027400156527)
XLA Ops:
  8.0 0.8 stack.18
  8.8 8.6 %all-to-all-start = ((f32[16,67,128]{2,1,0:T(8,128)}), f32[16,67,128]{2,1,0:T(8,128)S(1)}, u32[]{:S(2)}, u32[]{:S(2)}) async-start(f32[16,67,128]{2,1,0:T(8,128)} %stack.18), calls=%async_computation | async-start | bytes 1179648 | tf_op jit(solution)/shard_map/all_to_all | solution.py:12
  17.5 26.6 %all_gather.6 = f32[67,2048]{1,0:T(8,128)S(1)} all-gather(f32[67,128]{1,0:T(8,128)S(1)} %pad_maximum_fusion), channel_id=1, replica_groups=mesh['row'=16,'col'=16] {'row'}, dimensions={1}, use_global_device_ids=true | all-gather | bytes 583168 | tf_op jit(solution)/shard_map/all_gather | solution.py:33
  45.0 29.3 %while.57 = (s32[]{:T(128)}, f32[8,1,256]{2,1,0:T(1,128)S(1)}, s32[8]{0:T(128)S(1)}, s32[2048]{0:T(1024)S(1)}, f32[2048]{0:T(1024)S(1)}, /*index=5*/f32[2048]{0:...) while((s32[]{:T(128)}, f32[8,1,256]{2,1,0:T(1,128)S(1)}, ...), condition=%wide.region_4.5_spmd.clone, body=%wide.region_2.4_spmd.clone.sunk | while | flops 406353664 | bytes 623819 | solution.py:80
  46.3 2.3 fusion.129
  49.9 2.3 fusion.129
  53.6 2.3 fusion.129
  57.3 2.3 fusion.129
  60.9 2.3 fusion.129
  64.6 2.3 fusion.129
  68.3 2.3 fusion.129
  71.9 2.3 fusion.129
  74.3 45.2 %pmin.7 = f32[2048]{0:T(1024)S(1)} all-reduce(f32[2048]{0:T(1024)S(1)} %bitcast.148), channel_id=1, replica_groups=mesh['row'=16,'col'=16] {'col'}, use_global_device_ids=true, to_apply=%region_5.6 | all-reduce | flops 2048 | bytes 16384 | tf_op jit(solution)/shard_map/pmin | solution.py:89
  119.6 34.9 %while.58 = (s32[]{:T(128)}, f32[8,3,256]{2,1,0:T(4,128)S(1)}, s32[8]{0:T(128)S(1)}, s32[2048]{0:T(1024)S(1)}, f32[2048]{0:T(1024)S(1)}, /*index=5*/f32[2048]{0:...) while((s32[]{:T(128)}, f32[8,3,256]{2,1,0:T(4,128)S(1)}, ...), condition=%wide.region_10.11_spmd.clone, body=%wide.region_6.10_spmd.clone.sunk | while | flops 409500672 | bytes 637155 | solution.py:80
  121.0 2.9 fusion.132
  125.4 2.9 fusion.132
  129.8 2.9 fusion.132
  134.1 2.9 fusion.132
  138.5 2.9 fusion.132
  142.9 2.9 fusion.132
  147.2 2.9 fusion.132
  151.6 2.9 fusion.132
  154.6 74.6 %all-reduce = (f32[2048]{0:T(1024)S(1)}, f32[2048]{0:T(1024)S(1)}, f32[2048]{0:T(1024)S(1)}) all-reduce(f32[2048]{0:T(1024)S(1)} %bitcast.146, f32[2048]{0:T(1024)S(1)} %bitcast.147, f32[2048]{0:T(1024)S(1)} %bitcast.145), channel_id=1, replica_groups=mesh['row'=16,'col'=16] {'col'}, use_global_device_ids=true, to_apply=%region_12.13 | all-reduce | flops 6144 | bytes 49152 | tf_op jit(solution)/shard_map/psum | solution.py:105
  229.3 32.6 %while.59 = (s32[]{:T(128)}, f32[8,1,256]{2,1,0:T(1,128)S(1)}, s32[8]{0:T(128)S(1)}, s32[2048]{0:T(1024)S(1)}, f32[2048]{0:T(1024)S(1)}, /*index=5*/f32[2048]{0:...) while((s32[]{:T(128)}, f32[8,1,256]{2,1,0:T(1,128)S(1)}, ...), condition=%wide.region_16.17_spmd.clone, body=%wide.region_14.16_spmd.clone.sunk | while | flops 407402496 | bytes 629987 | solution.py:80
  230.8 2.6 fusion.137
  234.8 2.6 fusion.137
  238.9 2.6 fusion.137
  243.0 2.6 fusion.137
  247.1 2.6 fusion.137
  251.1 2.6 fusion.137
  255.2 2.6 fusion.137
  259.3 2.6 fusion.137
  261.9 38.8 %psum.38 = f32[2048]{0:T(1024)S(1)} all-reduce(f32[2048]{0:T(1024)S(1)} %bitcast.149), channel_id=1, replica_groups=mesh['row'=16,'col'=16] {'col'}, use_global_device_ids=true, to_apply=%region_17.18 | all-reduce | flops 2048 | bytes 16384 | tf_op jit(solution)/shard_map/psum | solution.py:118
  300.8 28.0 %all_gather.7 = f32[3,2048]{1,0:T(4,128)S(1)} all-gather(f32[3,128]{1,0:T(4,128)S(1)} %pad_maximum_fusion.1), channel_id=1, replica_groups=mesh['row'=16,'col'=16] {'row'}, dimensions={1}, use_global_device_ids=true | all-gather | bytes 26112 | tf_op jit(solution)/shard_map/all_gather | solution.py:126
  328.9 34.7 %while.60 = (s32[]{:T(128)}, f32[]{:T(128)}, s32[8]{0:T(128)S(1)}, s32[2048]{0:T(1024)S(1)}, f32[2,2048]{1,0:T(2,128)S(1)}, /*index=5*/f32[2,2048]{1,0:T(2,128)S...) while((s32[]{:T(128)}, f32[]{:T(128)}, s32[8]{0:T(128)S(1)}, ...), condition=%wide.region_20.21_spmd.clone, body=%wide.region_18.20_spmd.clone.sunk | while | flops 5273607 | bytes 74971 | solution.py:137
  330.5 2.1 select_reduce_fusion.2
  334.8 2.1 select_reduce_fusion.2
  339.2 2.1 select_reduce_fusion.2
  343.5 2.1 select_reduce_fusion.2
  347.8 2.1 select_reduce_fusion.2
  352.2 2.1 select_reduce_fusion.2
  356.5 2.1 select_reduce_fusion.2
  360.9 2.1 select_reduce_fusion.2
  363.6 77.2 %psum.39 = f32[]{:T(128)} all-reduce(f32[]{:T(128)} %get-tuple-element.407), channel_id=1, replica_groups=mesh['row'=16,'col'=16] {'row','col'}, use_global_device_ids=true, to_apply=%region_21.22 | all-reduce | flops 1 | bytes 8 | tf_op jit(solution)/shard_map/psum | solution.py:140
  440.9 65.5 %while.61 = (s32[]{:T(128)}, f32[8,2,256]{2,1,0:T(2,128)S(1)}, s32[8]{0:T(128)S(1)}, f32[2,2048]{1,0:T(2,128)S(1)}, s32[2048]{0:T(1024)S(1)}, /*index=5*/f32[204...) while((s32[]{:T(128)}, f32[8,2,256]{2,1,0:T(2,128)S(1)}, ...), condition=%wide.region_24.25_spmd.clone, body=%wide.region_22.24_spmd.clone.sunk | while | flops 429423616 | bytes 4926787 | solution.py:80
  442.7 4.6 fusion.145
  447.3 1.7 fusion.146
  450.9 4.6 fusion.145
  455.5 1.7 fusion.146
  459.1 4.6 fusion.145
  463.7 1.7 fusion.146
  467.3 4.6 fusion.145
  471.9 1.7 fusion.146
  475.5 4.6 fusion.145
  480.1 1.7 fusion.146
  483.7 4.6 fusion.145
  488.3 1.7 fusion.146
  491.9 4.6 fusion.145
  496.5 1.7 fusion.146
  500.1 4.6 fusion.145
  504.7 1.7 fusion.146
  506.4 1.4 copy.11
  508.4 84.2 %reduce-scatter.4.cloned.1.call-done = f32[128,2]{1,0:T(8,128)} async-done(((f32[2048,2]{1,0:T(8,128)}), f32[128,2]{1,0:T(8,128)}) %reduce-scatter.4.cloned.1.call-update) | async-done | bytes 1040
  592.6 1.5 copy.12
  (295 shorter events, 38.9 us)
Async XLA Ops:
  8.8 35.4 %all-to-all-start = ((f32[16,67,128]{2,1,0:T(8,128)}), f32[16,67,128]{2,1,0:T(8,128)S(1)}, u32[]{:S(2)}, u32[]{:S(2)}) async-start(f32[16,67,128]{2,1,0:T(8,128)} %stack.18), calls=%async_computation | async-start | bytes 1179648 | tf_op jit(solution)/shard_map/all_to_all | solution.py:12
  17.5 575.2 %reduce-scatter.4.cloned.1.call-start = ((), (), s32[]{:S(2)}) async-start(), calls=%async_computation.2 | async-start | bytes 1114112
  44.2 0.8 copy-start
  229.3 99.6 %slice-start = ((f32[67,2048]{1,0:T(8,128)}), f32[2,2048]{1,0:T(2,128)S(1)}, s32[]{:S(2)}) async-start(f32[67,2048]{1,0:T(8,128)} %copy-done), calls=%async_computation.3 | async-start | bytes 32768 | tf_op jit(solution)/shard_map/slice | solution.py:40
Sparse Core Ops, SparseCore 0:
  507.9 84.6 reduce-scatter.3
